TPU v7x, 128 devices: a whole 4x4x4 slice. The times are simulated.
128 devices in a mesh: req: 32 (over z, x, core), mlp: 4 (over y).
Axes of the slice: x: 4, y: 4, z: 4, core: 2. Of those that a mesh axis runs over, the one named last changes fastest.
Arguments:
- tokens: bfloat16 [12288, 2048], P(('req', 'mlp')), may hold values from -6 to 6
- lengths: int32 [4], replicated, may hold values from 1 to 6144, 12288 in all
- in_gain: float32 [2048], replicated, may hold values from 0.5 to 1.5
- w_query: bfloat16 [2048, 2048], P(None, 'mlp'), may hold values from -0.125 to 0.125
- w_key: bfloat16 [2048, 2048], P(None, 'mlp'), may hold values from -1 to 1
- w_value: bfloat16 [2048, 4096], P(None, 'mlp'), may hold values from -0.125 to 0.125
- w_gate: bfloat16 [2048, 4096], P(None, 'mlp'), may hold values from -0.125 to 0.125
- w_beta: bfloat16 [2048, 16], P(None, 'mlp'), may hold values from -0.125 to 0.125
- w_decay: bfloat16 [2048, 16], P(None, 'mlp'), may hold values from -0.125 to 0.125
- decay_log: float32 [16], P('mlp'), may hold values from -11 to 0
- decay_bias: float32 [16], P('mlp'), may hold values from -3 to 1
- conv_query: float32 [4, 2048], P(None, 'mlp'), may hold values from -2.5 to 2.5
- conv_key: float32 [4, 2048], P(None, 'mlp'), may hold values from -2.5 to 2.5
- conv_value: float32 [4, 4096], P(None, 'mlp'), may hold values from -2.5 to 2.5
- head_gain: float32 [256], replicated, may hold values from 0.5 to 1.5
- w_out: bfloat16 [4096, 2048], P('mlp'), may hold values from -0.09375 to 0.09375
- mlp_gain: float32 [2048], replicated, may hold values from 0.5 to 1.5
- w_up_gate: bfloat16 [2048, 5632], P('req', 'mlp'), may hold values from -0.125 to 0.125
- w_up: bfloat16 [2048, 5632], P('req', 'mlp'), may hold values from -0.125 to 0.125
- w_down: bfloat16 [5632, 2048], P('mlp', 'req'), may hold values from -0.078125 to 0.078125
Outputs:
- layer_out: bfloat16 [12288, 2048], P(('req', 'mlp'))
Inputs may be any that keep to these rules, and one draw needn't show every extreme that they name: The 4 prompts lie end to end in the order given and their lengths sum to 12288; the longest has exactly 6144 tokens.
All inputs are finite; a program needn't handle non-finite values.
Results may differ from a plain program's by a relative error of at most 0.017.
Values may be sent and summed in bfloat16 or wider, within the bound.
No kernel may reach another device: no remote copies, remote signals or barrier semaphores. Data moves between devices by JAX's collectives and lax.ppermute only.
A program may use at most 128 MiB of HBM per device.

v0:
```python
import jax
import jax.numpy as jnp
from jax import lax
from jax.sharding import PartitionSpec as P

GROUP = 64
maximal_matmul_accuracy = lax.Precision.HIGHEST


def shifted(value, axis, steps):
    count = lax.axis_size(axis)
    first, last = (max(0, -steps), min(count, count - steps))
    return lax.ppermute(value, axis, [(source, source + steps) for source in range(first, last)])


def carried_in(shard, axis, combine, identity):
    length, index = (lax.axis_size(axis), lax.axis_index(axis))
    everything = jax.tree.map(
        lambda part, kind: lax.all_gather(part.astype(kind), axis),
        shard,
        jax.tree.map(lambda a: jnp.bfloat16 if a.dtype == jnp.float32 else a.dtype, shard),
    )
    start = jax.tree.map(
        lambda part, zero: jnp.broadcast_to(jnp.asarray(zero, part.dtype), part.shape),
        shard,
        identity,
    )

    def step(k, before):
        reached = k < index
        new = combine(
            before, jax.tree.map(lambda part, own: part[k].astype(own.dtype), everything, shard)
        )
        return jax.tree.map(lambda a, b: jnp.where(reached, a, b), new, before)

    return lax.fori_loop(0, length, step, start)


def rms_scale(values, gain):
    mean_square = jnp.mean(values * values, axis=-1, keepdims=True)
    return values / jnp.sqrt(mean_square + 1e-06) * gain


def unit_norm(values):
    return values / jnp.sqrt(jnp.sum(values * values, axis=-1, keepdims=True) + 1e-06)


def segment_of(positions, lengths):
    bounds = jnp.cumsum(lengths)[:-1]
    return jnp.sum((positions[:, None] >= bounds[None, :]).astype(jnp.int32), axis=1)


def causal_conv(projected, rim_rows, kernel, segment_ids, rim_segments):
    taps_count = kernel.shape[0]
    row_count = projected.shape[0]
    extended = jnp.concatenate([rim_rows, projected], axis=0).astype(jnp.float32)
    extended_ids = jnp.concatenate([rim_segments, segment_ids], axis=0)
    accumulated = jnp.zeros(projected.shape, jnp.float32)
    for offset in range(taps_count):
        window = lax.slice_in_dim(extended, offset, offset + row_count, axis=0)
        window_ids = lax.slice_in_dim(extended_ids, offset, offset + row_count, axis=0)
        same_doc = (window_ids == segment_ids)[:, None]
        accumulated = accumulated + kernel[offset][None, :] * jnp.where(same_doc, window, 0.0)
    return accumulated


def group_parts(query_vecs, key_vecs, value_vecs, beta_vals, log_decay, segment_ids, prior_segment):
    group_rows = query_vecs.shape[0]
    value_dim = value_vecs.shape[-1]
    cumulative = jnp.cumsum(log_decay, axis=0)
    row_index = jnp.arange(group_rows)[:, None]
    col_index = jnp.arange(group_rows)[None, :]
    same_doc = segment_ids[:, None] == segment_ids[None, :]
    keep_mask = ((row_index >= col_index) & same_doc)[None, :, :]
    strict_mask = (row_index > col_index)[None, :, :]
    head_cumul = jnp.transpose(cumulative)
    gaps = head_cumul[:, :, None] - head_cumul[:, None, :]
    weights = jnp.where(keep_mask, jnp.exp(jnp.where(keep_mask, gaps, 0.0)), 0.0)
    open_mask = (segment_ids == prior_segment).astype(query_vecs.dtype)
    start_decay = jnp.exp(cumulative) * open_mask[:, None]
    key_dots = jnp.einsum("ihd,jhd->hij", key_vecs, key_vecs, precision=maximal_matmul_accuracy)
    coupling = jnp.where(
        strict_mask, jnp.transpose(beta_vals)[:, :, None] * weights * key_dots, 0.0
    )
    system = coupling + jnp.eye(group_rows, dtype=query_vecs.dtype)[None]
    targets = jnp.concatenate(
        [beta_vals[:, :, None] * value_vecs, (beta_vals * start_decay)[:, :, None] * key_vecs],
        axis=-1,
    )
    solved = jax.scipy.linalg.solve_triangular(
        system, jnp.transpose(targets, (1, 0, 2)), lower=True, unit_diagonal=True
    )
    starting_value_rows = solved[:, :, :value_dim]
    delta_correction = solved[:, :, value_dim:]
    query_dots = weights * jnp.einsum(
        "ihd,jhd->hij", query_vecs, key_vecs, precision=maximal_matmul_accuracy
    )
    query_begin_offset = query_vecs * start_decay[:, :, None]
    final_key_rows = key_vecs * jnp.transpose(weights[:, -1, :])[:, :, None]
    carried_decay_factor = start_decay[-1]
    return (
        starting_value_rows,
        delta_correction,
        query_dots,
        query_begin_offset,
        final_key_rows,
        carried_decay_factor,
    )


def group_step(running_state, parts):
    (
        starting_value_rows,
        delta_correction,
        query_dots,
        query_begin_offset,
        final_key_rows,
        carried_decay_factor,
    ) = parts
    fresh_state_update = starting_value_rows - jnp.einsum(
        "mxf,mft->mxt", delta_correction, running_state, precision=maximal_matmul_accuracy
    )
    output_rows = jnp.einsum(
        "fob,obt->fot", query_begin_offset, running_state, precision=maximal_matmul_accuracy
    )
    output_rows = output_rows + jnp.einsum(
        "hij,hjv->ihv", query_dots, fresh_state_update, precision=maximal_matmul_accuracy
    )
    updated_state = carried_decay_factor[:, None, None] * running_state + jnp.einsum(
        "new,enr->ewr", final_key_rows, fresh_state_update, precision=maximal_matmul_accuracy
    )
    return (updated_state, output_rows)


def combine_maps(earlier, later):
    earlier_map, preceding_additive = earlier
    following_linear_map, following_additive = later
    joined_map = jnp.einsum(
        "hkl,hlm->hkm", following_linear_map, earlier_map, precision=maximal_matmul_accuracy
    )
    joined_add = (
        jnp.einsum(
            "baf,bfu->bau",
            following_linear_map,
            preceding_additive,
            precision=maximal_matmul_accuracy,
        )
        + following_additive
    )
    return (joined_map, joined_add)


def per_device(
    tokens,
    lengths,
    in_gain,
    w_query,
    w_key,
    w_value,
    w_gate,
    w_beta,
    w_decay,
    decay_log,
    decay_bias,
    conv_query,
    conv_key,
    conv_value,
    head_gain,
    w_out,
    mlp_gain,
    w_up_gate,
    w_up,
    w_down,
):
    share_rows = tokens.shape[0]
    gathered = lax.all_gather(tokens, "mlp", axis=0, tiled=True)
    piece_len = gathered.shape[0]
    head_count = w_beta.shape[1]
    key_dim = w_query.shape[1] // head_count
    value_dim = w_value.shape[1] // head_count
    taps_count = conv_query.shape[0]
    group_count = piece_len // GROUP
    piece_start = lax.axis_index("req") * piece_len
    positions = piece_start + jnp.arange(piece_len, dtype=jnp.int32)
    segment_ids = segment_of(positions, lengths)
    rim_segments = segment_of(
        piece_start - (taps_count - 1) + jnp.arange(taps_count - 1, dtype=jnp.int32), lengths
    )
    token_rows = gathered.astype(jnp.float32)
    normed = rms_scale(token_rows, in_gain).astype(jnp.bfloat16)
    proj_query = jnp.dot(normed, w_query, preferred_element_type=jnp.float32).astype(jnp.bfloat16)
    proj_key = jnp.dot(normed, w_key, preferred_element_type=jnp.float32).astype(jnp.bfloat16)
    proj_value = jnp.dot(normed, w_value, preferred_element_type=jnp.float32).astype(jnp.bfloat16)
    edge_rows = jnp.concatenate(
        [
            proj_query[piece_len - taps_count + 1 :],
            proj_key[piece_len - taps_count + 1 :],
            proj_value[piece_len - taps_count + 1 :],
        ],
        axis=1,
    )
    rim_all = shifted(edge_rows, "req", 1)
    query_width = proj_query.shape[1]
    key_width = proj_key.shape[1]
    rim_query = rim_all[:, :query_width]
    rim_key = rim_all[:, query_width : query_width + key_width]
    rim_value = rim_all[:, query_width + key_width :]
    conv_q = jax.nn.silu(causal_conv(proj_query, rim_query, conv_query, segment_ids, rim_segments))
    conv_k = jax.nn.silu(causal_conv(proj_key, rim_key, conv_key, segment_ids, rim_segments))
    conv_v = jax.nn.silu(causal_conv(proj_value, rim_value, conv_value, segment_ids, rim_segments))
    query_vecs = unit_norm(conv_q.reshape(piece_len, head_count, key_dim)) * key_dim ** (-0.5)
    key_vecs = unit_norm(conv_k.reshape(piece_len, head_count, key_dim))
    value_vecs = conv_v.reshape(piece_len, head_count, value_dim)
    gate_lin = jnp.dot(normed, w_gate, preferred_element_type=jnp.float32).astype(jnp.bfloat16)
    beta_vals = jax.nn.sigmoid(jnp.dot(normed, w_beta, preferred_element_type=jnp.float32))
    log_decay = -jnp.exp(decay_log) * jax.nn.softplus(
        jnp.dot(normed, w_decay, preferred_element_type=jnp.float32) + decay_bias
    )

    def shaped(values):
        return values.reshape((group_count, GROUP) + values.shape[1:])

    prior_ids = segment_of(
        piece_start + jnp.arange(group_count, dtype=jnp.int32) * GROUP - 1, lengths
    )
    parts = jax.vmap(group_parts)(
        shaped(query_vecs),
        shaped(key_vecs),
        shaped(value_vecs),
        shaped(beta_vals),
        shaped(log_decay),
        shaped(segment_ids),
        prior_ids,
    )
    eye_block = jnp.broadcast_to(
        jnp.eye(key_dim, dtype=jnp.float32), (head_count, key_dim, key_dim)
    )
    zero_state = jnp.zeros((head_count, key_dim, value_dim), jnp.float32)

    def compose(carried, parts_one):
        (
            starting_value_rows,
            delta_correction,
            query_dots,
            query_begin_offset,
            final_key_rows,
            carried_decay_factor,
        ) = parts_one
        local_map = carried_decay_factor[:, None, None] * eye_block - jnp.einsum(
            "chk,hcl->hkl", final_key_rows, delta_correction, precision=maximal_matmul_accuracy
        )
        within_piece_additive = jnp.einsum(
            "new,enr->ewr", final_key_rows, starting_value_rows, precision=maximal_matmul_accuracy
        )
        return (combine_maps(carried, (local_map, within_piece_additive)), None)

    piece_maps, _ = lax.scan(compose, (eye_block, zero_state), parts)
    incoming = carried_in(piece_maps, "req", combine_maps, (eye_block, zero_state))
    _, output_rows = lax.scan(group_step, incoming[1], parts)
    output_rows = output_rows.reshape(piece_len, head_count, value_dim)
    gate_vals = jax.nn.silu(gate_lin.astype(jnp.float32)).reshape(piece_len, head_count, value_dim)
    head_out = (
        (rms_scale(output_rows, head_gain) * gate_vals)
        .reshape(piece_len, head_count * value_dim)
        .astype(jnp.bfloat16)
    )
    partial_out = jnp.dot(head_out, w_out, preferred_element_type=jnp.float32)
    attn_sum = lax.psum(partial_out.astype(jnp.bfloat16), "mlp").astype(jnp.float32)
    resid = token_rows + attn_sum
    mlp_in = rms_scale(resid, mlp_gain).astype(jnp.bfloat16)
    resid_mine = lax.dynamic_slice_in_dim(resid, lax.axis_index("mlp") * share_rows, share_rows, 0)

    def add_rows(piece):
        return jnp.dot(mlp_in, piece, preferred_element_type=jnp.float32)

    gate_acc = add_rows(lax.all_gather(w_up_gate, "req", axis=0, tiled=True))
    up_acc = add_rows(lax.all_gather(w_up, "req", axis=0, tiled=True))
    hidden = (jax.nn.silu(gate_acc) * up_acc).astype(jnp.bfloat16)
    down_terms = jnp.dot(
        hidden,
        lax.all_gather(w_down, "req", axis=1, tiled=True),
        preferred_element_type=jnp.float32,
    )
    mlp_share = lax.psum_scatter(
        down_terms.astype(jnp.bfloat16), "mlp", scatter_dimension=0, tiled=True
    ).astype(jnp.float32)
    return (resid_mine + mlp_share).astype(jnp.bfloat16)


def solution(mesh):
    placed = (
        P(("req", "mlp"), None),
        P(),
        P(),
        P(None, "mlp"),
        P(None, "mlp"),
        P(None, "mlp"),
        P(None, "mlp"),
        P(None, "mlp"),
        P(None, "mlp"),
        P("mlp"),
        P("mlp"),
        P(None, "mlp"),
        P(None, "mlp"),
        P(None, "mlp"),
        P(),
        P("mlp", None),
        P(),
        P("req", "mlp"),
        P("req", "mlp"),
        P("mlp", "req"),
    )
    return jax.shard_map(
        per_device, mesh=mesh, in_specs=placed, out_specs=P(("req", "mlp"), None), check_vma=False
    )
```

profile of v0, /device:TPU:0, one launch (start us, length us, event | category | flops | bytes accessed | tf_op | source)
XLA Modules:
  0.0 670.5 jit_solution(12898045852853135112)
XLA Ops:
  15.9 22.1 %all-gather.9.cloned.1.call-done = bf16[384,2048]{1,0:T(8,128)(2,1)} async-done(((bf16[96,2048]{1,0:T(8,128)(2,1)}), bf16[384,2048]{1,0:T(8,128)(2,1)}) %all-gather.9.cloned.1.call-update) | async-done | bytes 1572880 | tf_op jit(solution)/shard_map/all_gather | solution.py:176
  40.5 4.6 convolution_convert_fusion.3
  55.8 2.7 fusion.94
  61.0 2.8 fusion.64
  63.8 119.3 %custom-call.4 = f32[6,4,1,64,64]{3,4,2,1,0:T(8,128)} custom-call(f32[6,4,1,64,64]{4,3,2,1,0:T(8,128)} %fusion.64), custom_call_target="InvertDiagBlocksLowerTriangular" | custom-call | tf_op jit(solution)/shard_map/vmap(jit(_solve_triangular))/vmap()/triangular_solve | solution.py:90
  183.4 2.3 divide_multiply_fusion
  185.8 2.9 reshape_reshape.3
  194.9 23.6 %while.40 = (s32[]{:T(128)}, f32[4,128,128]{2,1,0:T(8,128)S(1)}, f32[4,128,256]{2,1,0:T(8,128)S(1)}, f32[6,4]{1,0:T(8,128)}, f32[6,64,4,128]{3,1,2,0:T(8,128)S(1...) while((s32[]{:T(128)}, f32[4,128,128]{2,1,0:T(8,128)S(1)}, ...), condition=%wide.region_8.9_spmd.clone, body=%wide.region_7.8_spmd.clone.sunk | while | flops 453378048 | bytes 4655763 | solution.py:257
  220.5 2.4 mul.377
  225.9 2.6 broadcast_multiply_fusion
  228.5 2.6 convolution_multiply_fusion.1
  231.1 35.7 %all-gather.17.cloned.1.call-done = bf16[128,128,128]{2,1,0:T(8,128)(2,1)} async-done(((bf16[4,128,128]{2,1,0:T(8,128)(2,1)}), bf16[128,128,128]{2,1,0:T(8,128)(2,1)}) %all-gather.17.cloned.1.call-update) | async-done | bytes 4194320 | tf_op jit(solution)/shard_map/all_gather | solution.py:19
  266.8 54.4 %all-gather.19.cloned.1.call-done = bf16[128,128,256]{2,1,0:T(8,128)(2,1)} async-done(((bf16[4,128,256]{2,1,0:T(8,128)(2,1)}), bf16[128,128,256]{2,1,0:T(8,128)(2,1)}) %all-gather.19.cloned.1.call-update) | async-done | bytes 8388624 | tf_op jit(solution)/shard_map/all_gather | solution.py:19
  321.3 50.3 %while.41 = (s32[]{:T(128)}, f32[4,128,256]{2,1,0:T(8,128)S(1)}, s32[]{:T(128)}, bf16[32,4,128,128]{3,2,1,0:T(8,128)(2,1)}, bf16[32,4,128,256]{3,2,1,0:T(8,128)(2,1)}, /*index=5*/s32[]{:T(128)}, s32[]{:T(128)}) while((s32[]{:T(128)}, f32[4,128,256]{2,1,0:T(8,128)S(1)}, s32[]{:T(128)}, bf16[32,4,128,128]{3,2,1,0:T(8,128)(2,1)}, ...), condition=%wide.region_10.11_spmd.clone, body=%wide.region_9.10_spmd.clone.sunk | while | flops 201981952 | bytes 3017311 | solution.py:36
  371.6 36.9 %while.39 = (s32[]{:T(128)}, f32[4,128,256]{2,1,0:T(8,128)S(1)}, f32[6,64,4,256]{3,1,2,0:T(8,128)}, f32[6,4]{1,0:T(8,128)}, f32[6,64,4,128]{3,1,2,0:T(8,128)S(1)...) while((s32[]{:T(128)}, f32[4,128,256]{2,1,0:T(8,128)S(1)}, ...), condition=%wide.region_13.14_spmd, body=%wide.region_12.13_spmd.sunk | while | flops 352714752 | bytes 4459661 | solution.py:259
  416.6 9.2 %convolution_convert_fusion.1 = bf16[384,2048]{1,0:T(8,128)(2,1)} fusion(bf16[1024,2048]{1,0:T(8,128)(2,1)} %param.41, f32[384,1024]{1,0:T(8,128)} %bitcast.169, f32[384,1024]{1,0:T(8,128)} %bitcast.168, bf16[384,2048]{1,0:T(8,128)(2,1)S(1)} %copy-done.5, bf16[2048,1024]{1,0:T(8,128)(2,1)} %param.32, f32[1024]{0:T(1024)S(1)} %bitcast.191), kind=kOutput, calls=%fused_computation.61 | convolution fusion | flops 3225944064 | bytes 14684160 | tf_op jit(solution)/shard_map/dot_general | solution.py:267
  428.0 47.9 %all-reduce.2.cloned.1.call-done = bf16[384,2048]{1,0:T(8,128)(2,1)} async-done(((bf16[384,2048]{1,0:T(8,128)(2,1)}), bf16[384,2048]{1,0:T(8,128)(2,1)}) %all-reduce.2.cloned.1.call-update) | async-done | bytes 1572880 | tf_op jit(solution)/shard_map/psum | solution.py:268
  475.9 3.5 convert_add_fusion
  479.4 46.8 %all-gather.11.cloned.1.call-done = bf16[2048,1408]{1,0:T(8,128)(2,1)} async-done(((bf16[64,1408]{1,0:T(8,128)(2,1)}), bf16[2048,1408]{1,0:T(8,128)(2,1)}) %all-gather.11.cloned.1.call-update) | async-done | bytes 5767184 | tf_op jit(solution)/shard_map/all_gather | solution.py:276
  526.2 7.2 %fusion.93 = f32[384,1408]{1,0:T(8,128)} fusion(bf16[2048,1408]{1,0:T(8,128)(2,1)} %all-gather.11.cloned.1.call-done, f32[2048]{0:T(1024)S(1)} %copy-done.42, f32[384]{0:T(512)S(1)} %add_sqrt_fusion.3, bf16[384,2048]{1,0:T(8,128)(2,1)} %all-reduce.2.cloned.1.call-done, bf16[384,2048]{1,0:T(8,128)(2,1)S(1)} %copy-done.3), kind=kOutput, calls=%fused_computation.178 | convolution fusion | flops 2219311104 | bytes 11085312 | tf_op jit(solution)/shard_map/dot_general | solution.py:274
  533.4 42.2 %all-gather.13.cloned.1.call-done = bf16[2048,1408]{1,0:T(8,128)(2,1)} async-done(((bf16[64,1408]{1,0:T(8,128)(2,1)}), bf16[2048,1408]{1,0:T(8,128)(2,1)}) %all-gather.13.cloned.1.call-update) | async-done | bytes 5767184 | tf_op jit(solution)/shard_map/all_gather | solution.py:277
  575.5 49.5 %all-gather.15.cloned.1.call-done = bf16[1408,2048]{0,1:T(8,128)(2,1)} async-done(((bf16[1408,64]{0,1:T(8,128)(2,1)}), bf16[1408,2048]{0,1:T(8,128)(2,1)}) %all-gather.15.cloned.1.call-update) | async-done | bytes 5767184 | tf_op jit(solution)/shard_map/all_gather | solution.py:281
  625.0 11.8 %convolution_convert_fusion = bf16[384,2048]{1,0:T(8,128)(2,1)} fusion(bf16[1408,2048]{0,1:T(8,128)(2,1)} %all-gather.15.cloned.1.call-done, bf16[2048,1408]{1,0:T(8,128)(2,1)} %all-gather.13.cloned.1.call-done, f32[384,1408]{1,0:T(8,128)} %fusion.93, f32[2048]{0:T(1024)S(1)} %copy-done.42, f32[384]{0:T(512)S(1)} %add_sqrt_fusion.3, ...), kind=kOutput, calls=%fused_computation.60 | convolution fusion | flops 4437934080 | bytes 18425344 | tf_op jit(solution)/shard_map/dot_general | solution.py:279
  636.8 24.7 %reduce-scatter.2.cloned.1.call-done = bf16[96,2048]{1,0:T(8,128)(2,1)} async-done(((bf16[384,2048]{1,0:T(8,128)(2,1)}), bf16[96,2048]{1,0:T(8,128)(2,1)}) %reduce-scatter.2.cloned.1.call-update) | async-done | bytes 393232 | tf_op jit(solution)/shard_map/reduce_scatter | solution.py:284
  (318 shorter events, 157.1 us)
Async XLA Ops:
  6.5 38.6 %copy-start = (bf16[2048,512]{1,0:T(8,128)(2,1)S(1)}, bf16[2048,512]{1,0:T(8,128)(2,1)}, u32[]{:S(2)}) copy-start(bf16[2048,512]{1,0:T(8,128)(2,1)} %param.29) | copy-start | bytes 6291460
  6.5 33.4 %copy-start.25 = (f32[2048]{0:T(1024)S(1)}, f32[2048]{0:T(1024)}, u32[]{:S(2)}) copy-start(f32[2048]{0:T(1024)} %param.28) | copy-start | bytes 24580
  6.5 31.5 %all-gather.9.cloned.1.call-start = ((), (), s32[]{:S(2)}) async-start(), calls=%async_computation.1 | async-start | bytes 1966080 | tf_op jit(solution)/shard_map/all_gather | solution.py:176
  7.3 259.6 %all-gather.17.cloned.1.call-start = ((), (), s32[]{:S(2)}) async-start(), calls=%async_computation.7 | async-start | bytes 4325376 | tf_op jit(solution)/shard_map/all_gather | solution.py:19
  40.5 9.1 %copy-start.4 = (bf16[384,2048]{1,0:T(8,128)(2,1)}, bf16[384,2048]{1,0:T(8,128)(2,1)S(1)}, u32[]{:S(2)}) copy-start(bf16[384,2048]{1,0:T(8,128)(2,1)S(1)} %fusion.44) | copy-start | bytes 4718596
  47.0 2.7 copy-start.21
  47.0 2.7 copy-start.40
  48.0 2.7 copy-start.22
  48.0 6.3 collective-permute-start
  60.9 2.9 copy-start.11
  61.0 122.2 %copy-start.15 = (bf16[384,1024]{1,0:T(8,128)(2,1)S(1)}, bf16[384,1024]{1,0:T(8,128)(2,1)}, u32[]{:S(2)}) copy-start(bf16[384,1024]{1,0:T(8,128)(2,1)} %copy-done.14) | copy-start | bytes 2359300
  63.8 119.6 %copy-start.23 = (f32[1,1024]{1,0:T(1,128)S(1)}, f32[1,1024]{1,0:T(1,128)}, u32[]{:S(2)}) copy-start(f32[1,1024]{1,0:T(1,128)} %get-tuple-element.401) | copy-start | bytes 12292
  63.8 119.6 %copy-start.24 = (f32[1,1024]{1,0:T(1,128)S(1)}, f32[1,1024]{1,0:T(1,128)}, u32[]{:S(2)}) copy-start(f32[1,1024]{1,0:T(1,128)} %get-tuple-element.402) | copy-start | bytes 12292
  185.8 2.9 copy-start.12
  219.3 102.0 %all-gather.19.cloned.1.call-start = ((), (), s32[]{:S(2)}) async-start(), calls=%async_computation.8 | async-start | bytes 8650752 | tf_op jit(solution)/shard_map/all_gather | solution.py:19
  220.1 255.8 %all-reduce.2.cloned.1.call-start = ((), (), s32[]{:S(2)}) async-start(), calls=%async_computation.2 | async-start | bytes 3145728 | tf_op jit(solution)/shard_map/psum | solution.py:268
  220.5 4.2 copy-start.9
  425.7 50.1 %copy-start.3 = (bf16[384,2048]{1,0:T(8,128)(2,1)S(1)}, bf16[384,2048]{1,0:T(8,128)(2,1)}, u32[]{:S(2)}) copy-start(bf16[384,2048]{1,0:T(8,128)(2,1)} %all-gather.9.cloned.1.call-done) | copy-start | bytes 4718596
  425.8 100.4 %all-gather.11.cloned.1.call-start = ((), (), s32[]{:S(2)}) async-start(), calls=%async_computation.3 | async-start | bytes 5947392 | tf_op jit(solution)/shard_map/all_gather | solution.py:276
  426.4 149.2 %all-gather.13.cloned.1.call-start = ((), (), s32[]{:S(2)}) async-start(), calls=%async_computation.4 | async-start | bytes 5947392 | tf_op jit(solution)/shard_map/all_gather | solution.py:277
  426.9 198.1 %all-gather.15.cloned.1.call-start = ((), (), s32[]{:S(2)}) async-start(), calls=%async_computation.5 | async-start | bytes 5947392 | tf_op jit(solution)/shard_map/all_gather | solution.py:281
  427.7 98.5 %copy-start.42 = (f32[2048]{0:T(1024)S(1)}, f32[2048]{0:T(1024)}, u32[]{:S(2)}) copy-start(f32[2048]{0:T(1024)} %param.42) | copy-start | bytes 24580
  427.7 233.8 %reduce-scatter.2.cloned.1.call-start = ((), (), s32[]{:S(2)}) async-start(), calls=%async_computation.6 | async-start | bytes 1966080 | tf_op jit(solution)/shard_map/reduce_scatter | solution.py:284
  636.7 26.9 %copy-start.1 = (bf16[2048,512]{1,0:T(8,128)(2,1)S(1)}, bf16[2048,512]{1,0:T(8,128)(2,1)}, u32[]{:S(2)}) copy-start(bf16[2048,512]{1,0:T(8,128)(2,1)} %param.29) | copy-start | bytes 6291460
  (28 other events, 53.9 us)
Sparse Core Ops, SparseCore 0:
  9.0 28.9 all-gather.8
  219.4 47.3 all-gather.16
  269.1 52.1 all-gather.18
  425.9 49.9 all-reduce.1
  478.0 48.1 all-gather.10
  528.3 47.1 all-gather.12
  577.8 47.1 all-gather.14
  636.9 24.5 reduce-scatter.1
where the time goes:
time: 673 us; the launch traced here: 670 us
  waiting for transfers between devices  326 us (48%)
  other arithmetic  148 us (22%)
  matrix products  144 us (21%)
  local copies, waits for them, and re-layouts  33.9 us (5%)
  between operations  14.3 us (2%)
    another operation x2, other arithmetic, group_parts(): jax.scipy.linalg.solve_triangular(system, jnp.transpose(targets, (1, 0, 2...  119 us
    all_gather x2, waiting for transfers between devices, carried_in(): lax.all_gather(part.astype(kind), axis)  90.2 us
    dot_general x38, matrix products, combine_maps(): jnp.einsum('baf,bfu->bau', following_linear_map, preceding_additive, prec...  51.6 us
    all_gather x1, waiting for transfers between devices, per_device(): lax.all_gather(w_down, 'req', axis=1, tiled=True)  49.5 us
    psum x1, waiting for transfers between devices, per_device(): lax.psum(partial_out.astype(jnp.bfloat16), 'mlp').astype(jnp.float32)  47.9 us
    all_gather x1, waiting for transfers between devices, per_device(): gate_acc = add_rows(lax.all_gather(w_up_gate, 'req', axis=0, tiled=True))  46.8 us
    all_gather x1, waiting for transfers between devices, per_device(): up_acc = add_rows(lax.all_gather(w_up, 'req', axis=0, tiled=True))  42.2 us
    reduce_scatter x1, waiting for transfers between devices, per_device(): lax.psum_scatter(down_terms.astype(jnp.bfloat16), 'mlp', scatter_dimensio...  24.7 us
  transfers between devices with their start and end apart: 9, of which 8 were waited for; matrix products, arithmetic and copies ran while one was open for 5% of the time, Pallas kernels for 0%

commit v1 on v0

--- a/solution.py
+++ b/solution.py
@@ -5,6 +5,13 @@
 
 GROUP = 64
 maximal_matmul_accuracy = lax.Precision.HIGHEST
+
+
+def _step_on_object(buf, array_dim):
+    buf = jnp.moveaxis(buf, 0, array_dim)
+    r1 = buf.shape
+    b_next = buf.reshape(*r1[:array_dim], r1[array_dim] * r1[array_dim + 1], *r1[array_dim + 2 :])
+    return b_next
 
 
 def shifted(value, axis, steps):
@@ -173,7 +180,21 @@
     w_down,
 ):
     share_rows = tokens.shape[0]
-    gathered = lax.all_gather(tokens, "mlp", axis=0, tiled=True)
+    nd = lax.axis_size("mlp")
+    made = [(at, (at + 1) % nd) for at in range(nd)]
+    mid_arr, main = ([], [])
+    in_order = [(j0, u) for u, j0 in made]
+    ix = 0
+    while ix < nd - 1:
+        if ix % 2 == 0:
+            mid_arr.append(lax.ppermute(mid_arr[-1] if mid_arr else tokens, "mlp", made))
+        else:
+            main.append(lax.ppermute(main[-1] if main else tokens, "mlp", in_order))
+        ix += 1
+    row_out = jnp.stack([*mid_arr[::-1], tokens, *main], axis=0)
+    big = lax.axis_index("mlp") - len(mid_arr)
+    row_out = row_out[(jnp.arange(nd) - big) % nd]
+    gathered = _step_on_object(row_out, 0)
     piece_len = gathered.shape[0]
     head_count = w_beta.shape[1]
     key_dim = w_query.shape[1] // head_count

time: 673 us -> 672 us (level)
  waiting for transfers between devices: 326 us -> 312 us
    all_gather x1 -> x0, waiting for transfers between devices: 22.1 us -> none  [per_device(): gathered = lax.all_gather(tokens, 'mlp', axis=0, tiled=True)]
    ppermute x0 -> x3, waiting for transfers between devices: none -> 11.3 us  [the longest x2 11.3 us: per_device(): lax.ppermute(mid_arr[-1] if mid_arr else tokens, 'mlp', made)]
  transfers between devices with their start and end apart: 9 -> 11, of which waited for: 8 -> 9; matrix products, arithmetic and copies ran while one was open for 5% -> 6% of each run, Pallas kernels for 0% -> 0%
where the time goes in v1:
time: 672 us; the launch traced here: 669 us
  waiting for transfers between devices  312 us (46%)
  other arithmetic  154 us (23%)
  matrix products  144 us (21%)
  local copies, waits for them, and re-layouts  37.2 us (6%)
  between operations  14.3 us (2%)
    another operation x2, other arithmetic, group_parts(): jax.scipy.linalg.solve_triangular(system, jnp.transpose(targets, (1, 0, 2...  119 us
    all_gather x2, waiting for transfers between devices, carried_in(): lax.all_gather(part.astype(kind), axis)  90.4 us
    dot_general x38, matrix products, combine_maps(): jnp.einsum('baf,bfu->bau', following_linear_map, preceding_additive, prec...  51.6 us
    all_gather x1, waiting for transfers between devices, per_device(): lax.all_gather(w_down, 'req', axis=1, tiled=True)  49.3 us
    psum x1, waiting for transfers between devices, per_device(): lax.psum(partial_out.astype(jnp.bfloat16), 'mlp').astype(jnp.float32)  48 us
    all_gather x1, waiting for transfers between devices, per_device(): gate_acc = add_rows(lax.all_gather(w_up_gate, 'req', axis=0, tiled=True))  44.7 us
    all_gather x1, waiting for transfers between devices, per_device(): up_acc = add_rows(lax.all_gather(w_up, 'req', axis=0, tiled=True))  42.2 us
    reduce_scatter x1, waiting for transfers between devices, per_device(): lax.psum_scatter(down_terms.astype(jnp.bfloat16), 'mlp', scatter_dimensio...  24.8 us
  transfers between devices with their start and end apart: 11, of which 9 were waited for; matrix products, arithmetic and copies ran while one was open for 6% of the time, Pallas kernels for 0%

profile of v1, /device:TPU:0, one launch (start us, length us, event | category | flops | bytes accessed | tf_op | source)
XLA Modules:
  0.0 669.4 jit_solution(775620099718975421)
XLA Ops:
  19.5 11.1 %collective-permute-done.1 = bf16[96,2048]{1,0:T(8,128)(2,1)} collective-permute-done((bf16[96,2048]{1,0:T(8,128)(2,1)S(1)}, bf16[96,2048]{1,0:T(8,128)(2,1)}, u32[]{:S(2)}, u32[]{:S(2)}) %collective-permute-start.1) | collective-permute-done | bytes 393248 | tf_op jit(solution)/shard_map/ppermute | solution.py:190
  30.6 2.5 pad_maximum_fusion
  33.1 3.2 gather_fusion
  40.2 4.6 convolution_convert_fusion.3
  55.2 2.7 fusion.95
  60.4 2.8 fusion.64
  63.3 119.3 %custom-call.4 = f32[6,4,1,64,64]{3,4,2,1,0:T(8,128)} custom-call(f32[6,4,1,64,64]{4,3,2,1,0:T(8,128)} %fusion.64), custom_call_target="InvertDiagBlocksLowerTriangular" | custom-call | tf_op jit(solution)/shard_map/vmap(jit(_solve_triangular))/vmap()/triangular_solve | solution.py:97
  185.2 2.9 reshape_reshape.3
  194.4 23.6 %while.40 = (s32[]{:T(128)}, f32[4,128,128]{2,1,0:T(8,128)S(1)}, f32[4,128,256]{2,1,0:T(8,128)S(1)}, f32[6,4]{1,0:T(8,128)}, f32[6,64,4,128]{3,1,2,0:T(8,128)S(1...) while((s32[]{:T(128)}, f32[4,128,128]{2,1,0:T(8,128)S(1)}, ...), condition=%wide.region_8.9_spmd.clone, body=%wide.region_7.8_spmd.clone.sunk | while | flops 453378048 | bytes 4655763 | solution.py:278
  225.3 2.6 broadcast_multiply_fusion
  227.9 2.6 convolution_multiply_fusion.1
  230.5 36.0 %all-gather.14.cloned.1.call-done = bf16[128,128,128]{2,1,0:T(8,128)(2,1)} async-done(((bf16[4,128,128]{2,1,0:T(8,128)(2,1)}), bf16[128,128,128]{2,1,0:T(8,128)(2,1)}) %all-gather.14.cloned.1.call-update) | async-done | bytes 4194320 | tf_op jit(solution)/shard_map/all_gather | solution.py:26
  266.5 54.4 %all-gather.16.cloned.1.call-done = bf16[128,128,256]{2,1,0:T(8,128)(2,1)} async-done(((bf16[4,128,256]{2,1,0:T(8,128)(2,1)}), bf16[128,128,256]{2,1,0:T(8,128)(2,1)}) %all-gather.16.cloned.1.call-update) | async-done | bytes 8388624 | tf_op jit(solution)/shard_map/all_gather | solution.py:26
  320.9 50.3 %while.41 = (s32[]{:T(128)}, f32[4,128,256]{2,1,0:T(8,128)S(1)}, s32[]{:T(128)}, bf16[32,4,128,128]{3,2,1,0:T(8,128)(2,1)}, bf16[32,4,128,256]{3,2,1,0:T(8,128)(2,1)}, /*index=5*/s32[]{:T(128)}, s32[]{:T(128)}) while((s32[]{:T(128)}, f32[4,128,256]{2,1,0:T(8,128)S(1)}, s32[]{:T(128)}, bf16[32,4,128,128]{3,2,1,0:T(8,128)(2,1)}, ...), condition=%wide.region_10.11_spmd.clone, body=%wide.region_9.10_spmd.clone.sunk | while | flops 201981952 | bytes 3017311 | solution.py:43
  371.2 36.9 %while.39 = (s32[]{:T(128)}, f32[4,128,256]{2,1,0:T(8,128)S(1)}, f32[6,64,4,256]{3,1,2,0:T(8,128)}, f32[6,4]{1,0:T(8,128)}, f32[6,64,4,128]{3,1,2,0:T(8,128)S(1)...) while((s32[]{:T(128)}, f32[4,128,256]{2,1,0:T(8,128)S(1)}, ...), condition=%wide.region_13.14_spmd, body=%wide.region_12.13_spmd.sunk | while | flops 352714752 | bytes 4459661 | solution.py:280
  416.2 9.2 %convolution_convert_fusion.1 = bf16[384,2048]{1,0:T(8,128)(2,1)} fusion(bf16[1024,2048]{1,0:T(8,128)(2,1)} %param.41, f32[384,1024]{1,0:T(8,128)} %bitcast.188, f32[384,1024]{1,0:T(8,128)} %bitcast.187, bf16[384,2048]{1,0:T(8,128)(2,1)S(1)} %copy-done.4, bf16[2048,1024]{1,0:T(8,128)(2,1)} %param.32, f32[1024]{0:T(1024)S(1)} %bitcast.213), kind=kOutput, calls=%fused_computation.62 | convolution fusion | flops 3225944064 | bytes 14684160 | tf_op jit(solution)/shard_map/dot_general | solution.py:288
  427.5 48.0 %all-reduce.2.cloned.1.call-done = bf16[384,2048]{1,0:T(8,128)(2,1)} async-done(((bf16[384,2048]{1,0:T(8,128)(2,1)}), bf16[384,2048]{1,0:T(8,128)(2,1)}) %all-reduce.2.cloned.1.call-update) | async-done | bytes 1572880 | tf_op jit(solution)/shard_map/psum | solution.py:289
  475.5 3.7 bitcast_add_fusion
  481.1 44.7 %all-gather.8.cloned.1.call-done = bf16[2048,1408]{1,0:T(8,128)(2,1)} async-done(((bf16[64,1408]{1,0:T(8,128)(2,1)}), bf16[2048,1408]{1,0:T(8,128)(2,1)}) %all-gather.8.cloned.1.call-update) | async-done | bytes 5767184 | tf_op jit(solution)/shard_map/all_gather | solution.py:297
  525.8 7.1 %fusion.102 = f32[384,1408]{1,0:T(8,128)} fusion(bf16[384,2048]{1,0:T(8,128)(2,1)} %multiply_convert_fusion, bf16[2048,1408]{1,0:T(8,128)(2,1)} %all-gather.8.cloned.1.call-done), kind=kOutput, calls=%fused_computation.194 | convolution fusion | flops 2214592512 | bytes 9502720 | tf_op jit(solution)/shard_map/dot_general | solution.py:295
  532.9 42.2 %all-gather.10.cloned.1.call-done = bf16[2048,1408]{1,0:T(8,128)(2,1)} async-done(((bf16[64,1408]{1,0:T(8,128)(2,1)}), bf16[2048,1408]{1,0:T(8,128)(2,1)}) %all-gather.10.cloned.1.call-update) | async-done | bytes 5767184 | tf_op jit(solution)/shard_map/all_gather | solution.py:298
  575.1 49.3 %all-gather.12.cloned.1.call-done = bf16[1408,2048]{0,1:T(8,128)(2,1)} async-done(((bf16[1408,64]{0,1:T(8,128)(2,1)}), bf16[1408,2048]{0,1:T(8,128)(2,1)}) %all-gather.12.cloned.1.call-update) | async-done | bytes 5767184 | tf_op jit(solution)/shard_map/all_gather | solution.py:302
  624.5 11.2 %convolution_convert_fusion = bf16[384,2048]{1,0:T(8,128)(2,1)} fusion(bf16[1408,2048]{0,1:T(8,128)(2,1)} %all-gather.12.cloned.1.call-done, bf16[384,2048]{1,0:T(8,128)(2,1)S(1)} %copy-done.14, bf16[2048,1408]{1,0:T(8,128)(2,1)} %all-gather.10.cloned.1.call-done, f32[384,1408]{1,0:T(8,128)} %fusion.102), kind=kOutput, calls=%fused_computation.61 | convolution fusion | flops 4433215488 | bytes 16842752 | tf_op jit(solution)/shard_map/dot_general | solution.py:300
  635.7 24.8 %reduce-scatter.2.cloned.1.call-done = bf16[96,2048]{1,0:T(8,128)(2,1)} async-done(((bf16[384,2048]{1,0:T(8,128)(2,1)}), bf16[96,2048]{1,0:T(8,128)(2,1)}) %reduce-scatter.2.cloned.1.call-update) | async-done | bytes 393232 | tf_op jit(solution)/shard_map/reduce_scatter | solution.py:305
  (331 shorter events, 168.2 us)
Async XLA Ops:
  6.5 38.3 %copy-start = (bf16[2048,512]{1,0:T(8,128)(2,1)S(1)}, bf16[2048,512]{1,0:T(8,128)(2,1)}, u32[]{:S(2)}) copy-start(bf16[2048,512]{1,0:T(8,128)(2,1)} %param.29) | copy-start | bytes 6291460
  6.5 260.0 %all-gather.14.cloned.1.call-start = ((), (), s32[]{:S(2)}) async-start(), calls=%async_computation.6 | async-start | bytes 4325376 | tf_op jit(solution)/shard_map/all_gather | solution.py:26
  6.5 12.4 %collective-permute-start = (bf16[96,2048]{1,0:T(8,128)(2,1)}, bf16[96,2048]{1,0:T(8,128)(2,1)S(1)}, u32[]{:S(2)}, u32[]{:S(2)}) collective-permute-start(bf16[96,2048]{1,0:T(8,128)(2,1)} %param.26), channel_id=1, source_target_pairs={{0,1},{1,2},{2,3},{3,0},{4,5},{5,6},{6,7},{7,4},{8,9},{9,10},{10,1... | collective-permute-start | bytes 1179656 | tf_op jit(solution)/shard_map/ppermute | solution.py:190
  8.2 11.2 %collective-permute-start.2 = (bf16[96,2048]{1,0:T(8,128)(2,1)}, bf16[96,2048]{1,0:T(8,128)(2,1)S(1)}, u32[]{:S(2)}, u32[]{:S(2)}) collective-permute-start(bf16[96,2048]{1,0:T(8,128)(2,1)} %param.26), channel_id=1, source_target_pairs={{1,0},{2,1},{3,2},{0,3},{5,4},{6,5},{7,6},{4,7},{9,8},{10,9},{11,1... | collective-permute-start | bytes 1179656 | tf_op jit(solution)/shard_map/ppermute | solution.py:192
  19.0 11.6 %collective-permute-start.1 = (bf16[96,2048]{1,0:T(8,128)(2,1)S(1)}, bf16[96,2048]{1,0:T(8,128)(2,1)}, u32[]{:S(2)}, u32[]{:S(2)}) collective-permute-start(bf16[96,2048]{1,0:T(8,128)(2,1)S(1)} %collective-permute-done), channel_id=1, source_target_pairs={{0,1},{1,2},{2,3},{3,0},{4,5},{5,6},{6,7},{7,4},{8,9},{9,10},{10,1... | collective-permute-start | bytes 1179656 | tf_op jit(solution)/shard_map/ppermute | solution.py:190
  40.2 8.8 %copy-start.3 = (bf16[384,2048]{1,0:T(8,128)(2,1)}, bf16[384,2048]{1,0:T(8,128)(2,1)S(1)}, u32[]{:S(2)}) copy-start(bf16[384,2048]{1,0:T(8,128)(2,1)S(1)} %fusion.44) | copy-start | bytes 4718596
  47.7 6.0 collective-permute-start.3
  60.4 2.9 copy-start.11
  60.4 122.2 %copy-start.16 = (bf16[384,1024]{1,0:T(8,128)(2,1)S(1)}, bf16[384,1024]{1,0:T(8,128)(2,1)}, u32[]{:S(2)}) copy-start(bf16[384,1024]{1,0:T(8,128)(2,1)} %copy-done.15) | copy-start | bytes 2359300
  63.2 119.6 %copy-start.24 = (f32[1,1024]{1,0:T(1,128)S(1)}, f32[1,1024]{1,0:T(1,128)}, u32[]{:S(2)}) copy-start(f32[1,1024]{1,0:T(1,128)} %get-tuple-element.401) | copy-start | bytes 12292
  63.3 119.6 %copy-start.25 = (f32[1,1024]{1,0:T(1,128)S(1)}, f32[1,1024]{1,0:T(1,128)}, u32[]{:S(2)}) copy-start(f32[1,1024]{1,0:T(1,128)} %get-tuple-element.402) | copy-start | bytes 12292
  185.2 2.9 copy-start.12
  218.7 102.2 %all-gather.16.cloned.1.call-start = ((), (), s32[]{:S(2)}) async-start(), calls=%async_computation.7 | async-start | bytes 8650752 | tf_op jit(solution)/shard_map/all_gather | solution.py:26
  219.5 256.0 %all-reduce.2.cloned.1.call-start = ((), (), s32[]{:S(2)}) async-start(), calls=%async_computation.1 | async-start | bytes 3145728 | tf_op jit(solution)/shard_map/psum | solution.py:289
  220.0 4.2 copy-start.9
  425.4 50.1 %copy-start.2 = (bf16[4,96,2048]{2,1,0:T(8,128)(2,1)S(1)}, bf16[4,96,2048]{2,1,0:T(8,128)(2,1)}, u32[]{:S(2)}) copy-start(bf16[4,96,2048]{2,1,0:T(8,128)(2,1)} %gather_fusion) | copy-start | bytes 4718596
  425.4 100.4 %all-gather.8.cloned.1.call-start = ((), (), s32[]{:S(2)}) async-start(), calls=%async_computation.2 | async-start | bytes 5947392 | tf_op jit(solution)/shard_map/all_gather | solution.py:297
  426.0 149.1 %all-gather.10.cloned.1.call-start = ((), (), s32[]{:S(2)}) async-start(), calls=%async_computation.3 | async-start | bytes 5947392 | tf_op jit(solution)/shard_map/all_gather | solution.py:298
  426.6 197.9 %all-gather.12.cloned.1.call-start = ((), (), s32[]{:S(2)}) async-start(), calls=%async_computation.4 | async-start | bytes 5947392 | tf_op jit(solution)/shard_map/all_gather | solution.py:302
  427.1 52.0 %copy-start.27 = (f32[2048]{0:T(1024)S(1)}, f32[2048]{0:T(1024)}, u32[]{:S(2)}) copy-start(f32[2048]{0:T(1024)} %param.42) | copy-start | bytes 24580
  427.2 233.3 %reduce-scatter.2.cloned.1.call-start = ((), (), s32[]{:S(2)}) async-start(), calls=%async_computation.5 | async-start | bytes 1966080 | tf_op jit(solution)/shard_map/reduce_scatter | solution.py:305
  475.5 3.7 copy-start.8
  481.1 143.4 %copy-start.14 = (bf16[384,2048]{1,0:T(8,128)(2,1)S(1)}, bf16[384,2048]{1,0:T(8,128)(2,1)}, u32[]{:S(2)}) copy-start(bf16[384,2048]{1,0:T(8,128)(2,1)} %multiply_convert_fusion) | copy-start | bytes 4718596
  635.7 26.9 %copy-start.1 = (bf16[2048,512]{1,0:T(8,128)(2,1)S(1)}, bf16[2048,512]{1,0:T(8,128)(2,1)}, u32[]{:S(2)}) copy-start(bf16[2048,512]{1,0:T(8,128)(2,1)} %param.29) | copy-start | bytes 6291460
  (32 other events, 63.2 us)
Sparse Core Ops, SparseCore 0:
  218.8 47.6 all-gather.13
  268.8 52.1 all-gather.15
  425.5 49.9 all-reduce.1
  477.6 48.1 all-gather.7
  527.9 47.1 all-gather.9
  577.2 47.1 all-gather.11
  635.8 24.6 reduce-scatter.1
